TPU v7x, 256 devices: a whole 4x4x8 slice. The times are simulated.
256 devices in a mesh: dp: 16 (over z_lo, x), tensor: 16 (over y, z_hi, core).
Axes of the slice: x: 4, y: 4, z: 8 (z_hi: 2, z_lo: 4; z = z_hi * 4 + z_lo), core: 2. Of those that a mesh axis runs over, the one named last changes fastest.
Arguments:
- inner_x: bfloat16 [16, 2048, 7168], P('dp', None, 'tensor')
- gate_z: bfloat16 [16, 2048, 7168], P('dp', None, 'tensor'), may hold values from -6 to 6
- input_b: bfloat16 [16, 2048, 128], P('dp'), may hold values from -0.75 to 0.75
- output_c: bfloat16 [16, 2048, 128], P('dp'), may hold values from -6 to 6
- step_raw: float32 [16, 2048, 112], P('dp', None, 'tensor'), may hold values from -6 to 6
- decay_rate: float32 [112], P('tensor'), may hold values from 0.001 to 0.05
- skip_gain: float32 [112], P('tensor'), may hold values from 0.5 to 1.5
- norm_gain: float32 [7168], P('tensor'), may hold values from 0.5 to 1.5
- out_weight: bfloat16 [7168, 3584], P('tensor'), may hold values from -0.0625 to 0.0625
- segment: int32 [16, 2048], P('dp'), may hold values from 0 to 7, never falling along the last dimension, each value on 1 to 1024 neighbouring positions
- cache_slot: int32 [16, 8], replicated, may hold values from 0 to 127, as said below
Outputs:
- mixed: bfloat16 [16, 2048, 3584], P('dp', 'tensor')
- cache: float32 [128, 112, 4096], P('dp', 'tensor')
Inputs may be any that keep to these rules, and one draw needn't show every extreme that they name: `segment`: in each group's row the prompt numbers never fall and every prompt 0 to 7 is present. `cache_slot`: every slot is named exactly once; slot // 8 is the owning group, and no two prompts of one group have the same owning group.
All inputs are finite; a program needn't handle non-finite values.
Results may differ from a plain program's by a relative error of at most 0.018.
Values may be sent and summed in bfloat16 or wider, within the bound.
No kernel may reach another device: no remote copies, remote signals or barrier semaphores. Data moves between devices by JAX's collectives and lax.ppermute only.
A program may use at most 192 MiB of HBM per device.

v0:
```python
import jax
import jax.numpy as jnp
from jax import lax
from jax.sharding import PartitionSpec as P

HEADS = 112
HEAD = 64
STATE = 64
NGROUPS = 2
REQS = 8
BLOCK = 256
INNER = 7168
HIGHEST = lax.Precision.HIGHEST


def split_pair(values):
    upper = values.astype(jnp.bfloat16)
    lower = (values - upper.astype(jnp.float32)).astype(jnp.bfloat16)
    return (upper, lower)


def split_einsum(form, wide, narrow):
    upper, lower = split_pair(wide)
    first = jnp.einsum(form, upper, narrow, preferred_element_type=jnp.float32)
    return first + jnp.einsum(form, lower, narrow, preferred_element_type=jnp.float32)


def local(
    inner_x,
    gate_z,
    input_b,
    output_c,
    step_raw,
    decay_rate,
    skip_gain,
    norm_gain,
    out_weight,
    segment,
    cache_slot,
):
    stream_len = inner_x.shape[1]
    dev_width = inner_x.shape[2]
    dev_heads = decay_rate.shape[0]
    tensor_idx = lax.axis_index("tensor")
    group_idx = tensor_idx * dev_heads // (HEADS // NGROUPS)
    b_cols = lax.dynamic_slice_in_dim(input_b[0], group_idx * STATE, STATE, 1)
    c_cols = lax.dynamic_slice_in_dim(output_c[0], group_idx * STATE, STATE, 1)
    step_size = jax.nn.softplus(step_raw[0])
    cum_log = jnp.cumsum(-decay_rate[None, :] * step_size, axis=0)
    seg_row = segment[0]
    block_count = stream_len // BLOCK
    x_blk = inner_x[0].reshape(block_count, BLOCK, dev_heads, HEAD)
    cum_blk = cum_log.reshape(block_count, BLOCK, dev_heads)
    step_blk = step_size.reshape(block_count, BLOCK, dev_heads)
    seg_blk = seg_row.reshape(block_count, BLOCK)
    b_blk = b_cols.reshape(block_count, BLOCK, STATE)
    c_blk = c_cols.reshape(block_count, BLOCK, STATE)
    positions = jnp.arange(BLOCK)
    scores = jnp.einsum("btn,bsn->bts", c_blk, b_blk, preferred_element_type=jnp.float32)
    causal_mask = (positions[None, None, :] <= positions[None, :, None]) & (
        seg_blk[:, :, None] == seg_blk[:, None, :]
    )
    cum_t = cum_blk.transpose(0, 2, 1)
    log_gap = cum_t[:, :, :, None] - cum_t[:, :, None, :]
    weights = (
        jnp.exp(jnp.where(causal_mask[:, None], log_gap, -jnp.inf))
        * step_blk.transpose(0, 2, 1)[:, :, None, :]
        * scores[:, None]
    )
    intra_part = split_einsum("bhts,bshp->bthp", weights, x_blk)
    last_seg = seg_blk[:, -1]
    last_cum = cum_blk[:, -1]
    pull_back = (
        jnp.exp(last_cum[:, None, :] - cum_blk)
        * step_blk
        * (seg_blk == last_seg[:, None]).astype(jnp.float32)[:, :, None]
    )
    added = split_einsum("bshp,bsn->bhpn", pull_back[:, :, :, None] * x_blk, b_blk)
    prev_cum = jnp.concatenate([jnp.zeros((1, dev_heads), jnp.float32), last_cum[:-1]], axis=0)
    prev_seg = jnp.concatenate([jnp.full((1,), -1, seg_row.dtype), last_seg[:-1]], axis=0)
    blocks = jnp.arange(block_count)
    earlier = blocks[None, :] < blocks[:, None]
    mix_ok = earlier & (last_seg[None, :] == prev_seg[:, None])
    mix_gap = prev_cum[:, None, :] - last_cum[None, :, :]
    mix = jnp.exp(jnp.where(mix_ok[:, :, None], mix_gap, -jnp.inf))
    carried = jnp.sum(mix[:, :, :, None, None] * added[None], axis=1)
    live_rows = (seg_blk == prev_seg[:, None]).astype(jnp.float32)
    carry_decay = jnp.exp(cum_blk - prev_cum[:, None, :]) * live_rows[:, :, None]
    carry_part = split_einsum("bhpn,btn->bthp", carried, c_blk) * carry_decay[:, :, :, None]
    outputs = intra_part + carry_part + skip_gain[None, None, :, None] * x_blk.astype(jnp.float32)
    mixer_y = outputs.reshape(stream_len, dev_width)
    members = (seg_row[None, :] == jnp.arange(REQS)[:, None]).astype(jnp.float32)
    end_index = (
        jnp.sum((seg_row[None, :] <= jnp.arange(REQS)[:, None]).astype(jnp.int32), axis=1) - 1
    )
    at_end = (jnp.arange(stream_len)[None, :] == end_index[:, None]).astype(jnp.float32)
    end_cum = jnp.dot(at_end, cum_log, precision=HIGHEST)
    seg_end_cum = jnp.dot(members.T, end_cum, precision=HIGHEST)
    pull_all = jnp.exp(seg_end_cum - cum_log) * step_size
    weighted = (inner_x[0].reshape(stream_len, dev_heads, HEAD) * pull_all[:, :, None]).reshape(
        stream_len, dev_width
    )
    masked_b = (
        (members.astype(jnp.bfloat16)[:, :, None] * b_cols[None])
        .transpose(1, 0, 2)
        .reshape(stream_len, REQS * STATE)
    )
    finals = split_einsum("tc,tk->ck", weighted, masked_b)
    finals = (
        finals.reshape(dev_heads, HEAD, REQS, STATE)
        .transpose(2, 0, 1, 3)
        .reshape(REQS, dev_heads * HEAD * STATE)
    )
    gated = mixer_y * jax.nn.silu(gate_z[0].astype(jnp.float32))
    sum_sq = jnp.sum(gated * gated, axis=1)
    group_hot = (jnp.arange(NGROUPS) == group_idx).astype(jnp.float32)
    group_stat = lax.psum(sum_sq[:, None] * group_hot[None, :], "tensor")
    mean_sq = jnp.sum(group_stat * group_hot[None, :], axis=1) / (INNER // NGROUPS)
    rounded = (gated * lax.rsqrt(mean_sq + 1e-05)[:, None] * norm_gain[None, :]).astype(
        jnp.bfloat16
    )
    projected = lax.psum_scatter(
        jnp.dot(rounded, out_weight, preferred_element_type=jnp.float32).astype(jnp.bfloat16),
        "tensor",
        scatter_dimension=0,
        tiled=True,
    )
    mixed = projected[None]
    dp_idx = lax.axis_index("dp")
    dp_size = lax.axis_size("dp")
    own_slots = lax.dynamic_slice_in_dim(cache_slot, dp_idx, 1, 0)[0]
    dest_hot = ((own_slots // REQS)[:, None] == jnp.arange(dp_size)[None, :]).astype(jnp.float32)
    outbound = jnp.dot(dest_hot.T, finals, precision=HIGHEST).reshape(
        dp_size, dev_heads, HEAD * STATE
    )
    inbound = lax.all_to_all(
        outbound.astype(jnp.bfloat16), "dp", split_axis=0, concat_axis=0, tiled=True
    ).astype(outbound.dtype)
    wanted = dp_idx * REQS + jnp.arange(REQS)
    take_hot = jnp.any(cache_slot[:, :, None] == wanted[None, None, :], axis=1).astype(jnp.float32)
    cache = jnp.dot(
        take_hot.T, inbound.reshape(dp_size, dev_heads * HEAD * STATE), precision=HIGHEST
    )
    return (mixed, cache.reshape(REQS, dev_heads, HEAD * STATE))


def solution(mesh):
    in_specs = (
        P("dp", None, "tensor"),
        P("dp", None, "tensor"),
        P("dp", None, None),
        P("dp", None, None),
        P("dp", None, "tensor"),
        P("tensor"),
        P("tensor"),
        P("tensor"),
        P("tensor", None),
        P("dp", None),
        P(),
    )
    out_specs = (P("dp", "tensor", None), P("dp", "tensor", None))
    return jax.shard_map(local, mesh=mesh, in_specs=in_specs, out_specs=out_specs, check_vma=False)
```

profile of v0, /device:TPU:32, one launch (start us, length us, event | category | flops | bytes accessed | tf_op | source)
XLA Modules:
  0.0 360.7 jit_solution(5995153483289453547)
XLA Ops:
  7.8 1.4 reduce.9
  10.0 0.9 multiply_bitcast_fusion
  10.9 2.0 reduce-window.6
  14.3 0.9 dynamic-slice_reduce_fusion
  18.4 3.3 copy.177
  21.9 0.8 reduce.3
  22.8 2.5 constant_dynamic-slice_fusion
  25.3 1.2 copy.167
  26.7 1.0 copy.120
  27.6 1.3 compare_and_fusion
  28.9 1.5 fusion.46
  30.5 5.6 %fusion.4 = f32[8,7,256,64]{2,3,1,0:T(8,128)S(1)} fusion(f32[8,256,256]{2,1,0:T(8,128)S(1)} %fusion.46, f32[8,7,256]{2,1,0:T(8,128)S(1)} %get-tuple-element.6, f32[8,7,256]{2,1,0:T(8,128)S(1)} %copy.120, pred[8,256,256]{2,1,0:T(8,128)(4,1)S(1)} %compare_and_fusion, bf16[8,256,7,64]{1,0,3,2:T(8,128)(2,1)S(1)} %bitcast.162), kind=kOutput, calls=%fused_computation.7 | convolution fusion | flops 488112128 | bytes 8241152 | tf_op jit(solution)/shard_map/bhts,bshp->bthp/dot_general | solution.py:24
  36.1 6.2 %fusion.1 = f32[8,7,256,64]{2,3,1,0:T(8,128)S(1)} fusion(f32[8,256,256]{2,1,0:T(8,128)S(1)} %fusion.46, f32[8,7,256]{2,1,0:T(8,128)S(1)} %get-tuple-element.6, f32[8,7,256]{2,1,0:T(8,128)S(1)} %copy.120, pred[8,256,256]{2,1,0:T(8,128)(4,1)S(1)} %compare_and_fusion, bf16[8,256,7,64]{1,0,3,2:T(8,128)(2,1)S(1)} %bitcast.163), kind=kOutput, calls=%fused_computation.5 | convolution fusion | flops 499122176 | bytes 8241152 | tf_op jit(solution)/shard_map/bhts,bshp->bthp/dot_general | solution.py:25
  42.8 1.7 copy.179
  45.9 1.8 multiply_reduce_fusion
  48.3 2.8 multiply_reduce_fusion.1
  51.1 2.1 copy.144
  53.2 3.7 %copy.178 = f32[56,8,8,256]{3,1,2,0:T(8,128)} copy(f32[56,8,8,256]{3,2,1,0:T(8,128)S(1)} %bitcast.160) | data formatting | bytes 7340032
  57.0 92.2 %psum.7 = f32[2048,2]{0,1:T(2,128)S(1)} all-reduce(f32[2048,2]{0,1:T(2,128)S(1)} %broadcast_multiply_fusion.1), channel_id=1, replica_groups=mesh['dp'=16,'tensor'=16] {'tensor'}, use_global_device_ids=true, to_apply=%region_4.5 | all-reduce | flops 4096 | bytes 32768 | tf_op jit(solution)/shard_map/psum | solution.py:117
  149.3 15.2 %convolution_convert_fusion = bf16[2048,3584]{1,0:T(8,128)(2,1)} fusion(bf16[448,3584]{1,0:T(8,128)(2,1)S(1)} %copy-done, f32[2048,448]{0,1:T(8,128)} %bitcast.174, f32[448]{0:T(512)S(1)} %copy-done.15, f32[2048]{0:T(1024)S(1)} %add_rsqrt_fusion, bf16[1,2048,448]{1,2,0:T(8,128)(2,1)} %param.12), kind=kOutput, calls=%fused_computation | convolution fusion | flops 6592266240 | bytes 23406336 | tf_op jit(solution)/shard_map/dot_general | solution.py:123
  165.5 1.1 fusion.21
  167.6 1.1 fusion.66
  168.7 2.1 convolution_add_fusion
  170.8 2.7 reshape.333
  173.5 3.4 copy.237
  176.9 3.3 reshape.334
  180.2 2.3 convolution_convert_fusion.1
  182.6 1.5 copy.148
  184.1 6.5 %all-to-all-start = ((bf16[16,7,4096]{2,1,0:T(8,128)(2,1)}), bf16[16,7,4096]{2,1,0:T(8,128)(2,1)}, u32[]{:S(2)}, u32[]{:S(2)}) async-start(bf16[16,7,4096]{2,1,0:T(8,128)(2,1)} %copy.148), calls=%async_computation.1 | async-start | bytes 2097152 | tf_op jit(solution)/shard_map/all_to_all | solution.py:136
  190.7 17.8 %all-to-all-done = bf16[16,7,4096]{2,1,0:T(8,128)(2,1)} async-done(((bf16[16,7,4096]{2,1,0:T(8,128)(2,1)}), bf16[16,7,4096]{2,1,0:T(8,128)(2,1)}, u32[]{:S(2)}, u32[]{:S(2)}) %all-to-all-start) | async-done | bytes 917536 | tf_op jit(solution)/shard_map/all_to_all | solution.py:136
  208.5 3.2 fusion.39
  211.7 142.2 %reduce-scatter.2.cloned.1.call-done = bf16[128,3584]{1,0:T(8,128)(2,1)} async-done(((bf16[2048,3584]{1,0:T(8,128)(2,1)}), bf16[128,3584]{1,0:T(8,128)(2,1)}) %reduce-scatter.2.cloned.1.call-update) | async-done | bytes 917520 | tf_op jit(solution)/shard_map/reduce_scatter | solution.py:122
  (79 shorter events, 11.1 us)
Async XLA Ops:
  7.2 142.1 %copy-start = (bf16[448,3584]{1,0:T(8,128)(2,1)S(1)}, bf16[448,3584]{1,0:T(8,128)(2,1)}, u32[]{:S(2)}) copy-start(bf16[448,3584]{1,0:T(8,128)(2,1)} %param.19) | copy-start | bytes 9633796
  7.2 14.7 %copy-start.8 = (f32[1,2048,7]{1,0,2:T(1,128)S(1)}, f32[1,2048,7]{1,0,2:T(1,128)}, u32[]{:S(2)}) copy-start(f32[1,2048,7]{1,0,2:T(1,128)} %param.15) | copy-start | bytes 172036
  7.2 346.7 %reduce-scatter.2.cloned.1.call-start = ((), (), s32[]{:S(2)}) async-start(), calls=%async_computation.2 | async-start | bytes 15597568 | tf_op jit(solution)/shard_map/reduce_scatter | solution.py:122
  13.3 0.6 copy-start.5
  26.6 3.8 %copy-start.7 = (f32[2048,7]{0,1:T(8,128)S(1)}, f32[2048,7]{0,1:T(8,128)}, u32[]{:S(2)}) copy-start(f32[2048,7]{0,1:T(8,128)} %reduce.3) | copy-start | bytes 172036
  26.6 3.8 %copy-start.10 = (f32[8,256]{1,0:T(8,128)S(1)}, f32[8,256]{1,0:T(8,128)}, u32[]{:S(2)}) copy-start(f32[8,256]{1,0:T(8,128)} %get-tuple-element.7) | copy-start | bytes 24580
  26.6 3.8 %copy-start.11 = (f32[8,256]{1,0:T(8,128)S(1)}, f32[8,256]{1,0:T(8,128)}, u32[]{:S(2)}) copy-start(f32[8,256]{1,0:T(8,128)} %get-tuple-element.8) | copy-start | bytes 24580
  26.6 3.9 %copy-start.1 = (bf16[56,8,8,256]{3,2,1,0:T(8,128)(2,1)S(1)}, bf16[56,8,8,256]{3,2,1,0:T(8,128)(2,1)}, u32[]{:S(2)}) copy-start(bf16[56,8,8,256]{3,2,1,0:T(8,128)(2,1)} %copy.177) | copy-start | bytes 5505028
  36.1 6.2 %copy-start.4 = (bf16[1,2048,448]{1,2,0:T(8,128)(2,1)S(1)}, bf16[1,2048,448]{1,2,0:T(8,128)(2,1)}, u32[]{:S(2)}) copy-start(bf16[1,2048,448]{1,2,0:T(8,128)(2,1)} %param.12) | copy-start | bytes 5505028
  45.1 0.7 copy-start.13
  45.1 2.5 copy-start.3
  47.7 0.7 copy-start.16
  53.2 96.1 %copy-start.15 = (f32[448]{0:T(512)S(1)}, f32[448]{0:T(512)}, u32[]{:S(2)}) copy-start(f32[448]{0:T(512)} %param.18) | copy-start | bytes 5380
  164.5 0.7 copy-start.9
  164.5 0.8 copy-start.6
  164.5 2.3 copy-start.2
  173.5 6.7 %copy-start.14 = (s32[8]{0:T(128)S(1)}, s32[8]{0:T(128)}, u32[]{:S(2)}) copy-start(s32[8]{0:T(128)} %get-tuple-element.11) | copy-start | bytes 100
  176.9 13.7 %copy-start.12 = (s32[16,8]{0,1:T(8,128)S(1)}, s32[16,8]{0,1:T(8,128)}, u32[]{:S(2)}) copy-start(s32[16,8]{0,1:T(8,128)} %param.21) | copy-start | bytes 1540
  184.1 24.4 %all-to-all-start = ((bf16[16,7,4096]{2,1,0:T(8,128)(2,1)}), bf16[16,7,4096]{2,1,0:T(8,128)(2,1)}, u32[]{:S(2)}, u32[]{:S(2)}) async-start(bf16[16,7,4096]{2,1,0:T(8,128)(2,1)} %copy.148), calls=%async_computation.1 | async-start | bytes 2097152 | tf_op jit(solution)/shard_map/all_to_all | solution.py:136
Sparse Core Ops, SparseCore 0:
  164.6 189.2 reduce-scatter.1
where the time goes:
time: 361 us
  waiting for transfers between devices  160 us (44%)
  blocking collectives  92.2 us (26%)
  matrix products  43.2 us (12%)
  local copies, waits for them, and re-layouts  30.9 us (9%)
  between operations  14.4 us (4%)
  other arithmetic  13.5 us (4%)
  starting transfers between devices  6.55 us (2%)
    reduce_scatter x1, waiting for transfers between devices, local(): lax.psum_scatter(jnp.dot(rounded, out_weight, preferred_element_type=jnp....  142 us
    psum x1, blocking collectives, local(): group_stat = lax.psum(sum_sq[:, None] * group_hot[None, :], 'tensor')  92.2 us
    all_to_all x1, waiting for transfers between devices, local(): lax.all_to_all(outbound.astype(jnp.bfloat16), 'dp', split_axis=0, concat_...  17.8 us
    dot_general x1, matrix products, local(): jnp.dot(rounded, out_weight, preferred_element_type=jnp.float32)  15.2 us
    unnamed x49, local copies, waits for them, and re-layouts  13 us
    dot_general x4, matrix products, split_einsum(): jnp.einsum(form, lower, narrow, preferred_element_type=jnp.float32)  11.7 us
    dot_general x4, matrix products, split_einsum(): first = jnp.einsum(form, upper, narrow, preferred_element_type=jnp.float32)  7.99 us
  transfers between devices with their start and end apart: 2, of which 2 were waited for; matrix products, arithmetic and copies ran while one was open for 6% of the time, Pallas kernels for 0%

commit v1 on v0

--- a/solution.py
+++ b/solution.py
@@ -114,7 +114,7 @@
     gated = mixer_y * jax.nn.silu(gate_z[0].astype(jnp.float32))
     sum_sq = jnp.sum(gated * gated, axis=1)
     group_hot = (jnp.arange(NGROUPS) == group_idx).astype(jnp.float32)
-    group_stat = lax.psum(sum_sq[:, None] * group_hot[None, :], "tensor")
+    group_stat = jnp.sum(lax.all_gather(sum_sq[:, None] * group_hot[None, :], "tensor"), axis=0)
     mean_sq = jnp.sum(group_stat * group_hot[None, :], axis=1) / (INNER // NGROUPS)
     rounded = (gated * lax.rsqrt(mean_sq + 1e-05)[:, None] * norm_gain[None, :]).astype(
         jnp.bfloat16

time: 361 us -> 304 us (0.84)
  blocking collectives: 92.2 us -> 35 us
    psum x1 -> x0, blocking collectives: 92.2 us -> none  [local(): group_stat = lax.psum(sum_sq[:, None] * group_hot[None, :], 'tensor')]
    reduce_scatter x1, waiting for transfers between devices: 142 us -> 72.6 us  [local(): lax.psum_scatter(jnp.dot(rounded, out_weight, preferred_element_type=jnp....]
    all_to_all x1, waiting for transfers between devices: 17.8 us -> 85.6 us  [local(): lax.all_to_all(outbound.astype(jnp.bfloat16), 'dp', split_axis=0, concat_...]
    all_gather x0 -> x1, blocking collectives: none -> 35 us  [local(): lax.all_gather(sum_sq[:, None] * group_hot[None, :], 'tensor')]
  transfers between devices with their start and end apart: 2 -> 2, of which waited for: 2 -> 2; matrix products, arithmetic and copies ran while one was open for 6% -> 7% of each run, Pallas kernels for 0% -> 0%
where the time goes in v1:
time: 304 us; the launch traced here: 303 us
  waiting for transfers between devices  158 us (52%)
  matrix products  43.1 us (14%)
  blocking collectives  35 us (12%)
  local copies, waits for them, and re-layouts  30.9 us (10%)
  other arithmetic  14.6 us (5%)
  between operations  14.4 us (5%)
  starting transfers between devices  6.51 us (2%)
    all_to_all x1, waiting for transfers between devices, local(): lax.all_to_all(outbound.astype(jnp.bfloat16), 'dp', split_axis=0, concat_...  85.6 us
    reduce_scatter x1, waiting for transfers between devices, local(): lax.psum_scatter(jnp.dot(rounded, out_weight, preferred_element_type=jnp....  72.6 us
    all_gather x1, blocking collectives, local(): lax.all_gather(sum_sq[:, None] * group_hot[None, :], 'tensor')  35 us
    dot_general x1, matrix products, local(): jnp.dot(rounded, out_weight, preferred_element_type=jnp.float32)  15.2 us
    unnamed x49, local copies, waits for them, and re-layouts  13 us
    dot_general x4, matrix products, split_einsum(): jnp.einsum(form, lower, narrow, preferred_element_type=jnp.float32)  11.7 us
    dot_general x4, matrix products, split_einsum(): first = jnp.einsum(form, upper, narrow, preferred_element_type=jnp.float32)  7.99 us
    all_to_all x1, starting transfers between devices, local(): lax.all_to_all(outbound.astype(jnp.bfloat16), 'dp', split_axis=0, concat_...  6.47 us
  transfers between devices with their start and end apart: 2, of which 2 were waited for; matrix products, arithmetic and copies ran while one was open for 7% of the time, Pallas kernels for 0%

profile of v1, /device:TPU:32, one launch (start us, length us, event | category | flops | bytes accessed | tf_op | source)
XLA Modules:
  0.0 302.9 jit_solution(5617816239584312320)
XLA Ops:
  7.8 1.4 reduce.9
  10.0 0.9 multiply_bitcast_fusion
  10.9 2.0 reduce-window.6
  14.3 0.9 dynamic-slice_reduce_fusion
  18.4 3.3 %copy.208 = bf16[56,8,8,256]{3,2,1,0:T(8,128)(2,1)} copy(bf16[56,8,8,256]{3,1,2,0:T(8,128)(2,1)} %bitcast.168) | data formatting | bytes 3670016
  22.8 2.5 constant_dynamic-slice_fusion
  25.3 1.2 copy.198
  26.7 1.0 copy.151
  27.6 1.3 compare_and_fusion
  28.9 1.5 fusion.46
  30.5 5.6 %fusion.4 = f32[8,7,256,64]{2,3,1,0:T(8,128)S(1)} fusion(f32[8,256,256]{2,1,0:T(8,128)S(1)} %fusion.46, f32[8,7,256]{2,1,0:T(8,128)S(1)} %get-tuple-element.6, f32[8,7,256]{2,1,0:T(8,128)S(1)} %copy.151, pred[8,256,256]{2,1,0:T(8,128)(4,1)S(1)} %compare_and_fusion, bf16[8,256,7,64]{1,0,3,2:T(8,128)(2,1)S(1)} %bitcast.162), kind=kOutput, calls=%fused_computation.7 | convolution fusion | flops 488112128 | bytes 8241152 | tf_op jit(solution)/shard_map/bhts,bshp->bthp/dot_general | solution.py:24
  36.1 6.2 %fusion.1 = f32[8,7,256,64]{2,3,1,0:T(8,128)S(1)} fusion(f32[8,256,256]{2,1,0:T(8,128)S(1)} %fusion.46, f32[8,7,256]{2,1,0:T(8,128)S(1)} %get-tuple-element.6, f32[8,7,256]{2,1,0:T(8,128)S(1)} %copy.151, pred[8,256,256]{2,1,0:T(8,128)(4,1)S(1)} %compare_and_fusion, bf16[8,256,7,64]{1,0,3,2:T(8,128)(2,1)S(1)} %bitcast.163), kind=kOutput, calls=%fused_computation.5 | convolution fusion | flops 499122176 | bytes 8241152 | tf_op jit(solution)/shard_map/bhts,bshp->bthp/dot_general | solution.py:25
  42.8 1.7 copy.210
  45.9 1.8 multiply_reduce_fusion
  48.3 2.8 multiply_reduce_fusion.1
  51.1 2.1 copy.175
  53.2 3.7 %copy.209 = f32[56,8,8,256]{3,1,2,0:T(8,128)} copy(f32[56,8,8,256]{3,2,1,0:T(8,128)S(1)} %bitcast.160) | data formatting | bytes 7340032
  57.0 35.0 %all_gather.4 = f32[16,2048,2]{1,2,0:T(2,128)} all-gather(f32[1,2048,2]{1,2,0:T(2,128)S(1)} %broadcast_multiply_fusion.1), channel_id=1, replica_groups=mesh['dp'=16,'tensor'=16] {'tensor'}, dimensions={0}, use_global_device_ids=true | all-gather | bytes 278528 | tf_op jit(solution)/shard_map/all_gather | solution.py:117
  92.0 1.0 reduce_sum.47
  93.2 15.2 %convolution_convert_fusion = bf16[2048,3584]{1,0:T(8,128)(2,1)} fusion(bf16[448,3584]{1,0:T(8,128)(2,1)S(1)} %copy-done, f32[2048,448]{0,1:T(8,128)} %bitcast.174, f32[448]{0:T(512)S(1)} %copy-done.15, f32[2048]{0:T(1024)S(1)} %add_rsqrt_fusion, bf16[1,2048,448]{1,2,0:T(8,128)(2,1)} %param.12), kind=kOutput, calls=%fused_computation | convolution fusion | flops 6592266240 | bytes 23406336 | tf_op jit(solution)/shard_map/dot_general | solution.py:123
  109.4 1.1 fusion.21
  111.5 1.1 fusion.66
  112.6 2.1 convolution_add_fusion
  114.7 2.7 reshape.385
  117.4 3.5 %copy.268 = f32[7,64,8,64]{3,1,0,2:T(8,128)} copy(f32[7,64,8,64]{3,2,1,0:T(8,128)} %reshape.385) | data formatting | bytes 1835008 | tf_op jit(solution)/shard_map/reshape | solution.py:110
  120.8 3.4 %reshape.386 = f32[8,28672]{1,0:T(8,128)} reshape(f32[8,7,64,64]{3,2,1,0:T(8,128)} %bitcast.167) | data formatting | bytes 1835008 | tf_op jit(solution)/shard_map/reshape | solution.py:112
  124.2 2.3 convolution_convert_fusion.1
  126.5 1.5 copy.179
  128.0 6.5 %all-to-all-start = ((bf16[16,7,4096]{2,1,0:T(8,128)(2,1)}), bf16[16,7,4096]{2,1,0:T(8,128)(2,1)}, u32[]{:S(2)}, u32[]{:S(2)}) async-start(bf16[16,7,4096]{2,1,0:T(8,128)(2,1)} %copy.179), calls=%async_computation.1 | async-start | bytes 2097152 | tf_op jit(solution)/shard_map/all_to_all | solution.py:136
  134.6 85.6 %all-to-all-done = bf16[16,7,4096]{2,1,0:T(8,128)(2,1)} async-done(((bf16[16,7,4096]{2,1,0:T(8,128)(2,1)}), bf16[16,7,4096]{2,1,0:T(8,128)(2,1)}, u32[]{:S(2)}, u32[]{:S(2)}) %all-to-all-start) | async-done | bytes 917536 | tf_op jit(solution)/shard_map/all_to_all | solution.py:136
  220.2 3.2 %fusion.39 = f32[8,7,4096]{2,0,1:T(8,128)} fusion(pred[16,8]{0,1:T(8,128)(4,1)S(1)} %compare_reduce_fusion, bf16[2,8,7,4096]{3,2,1,0:T(8,128)(2,1)} %bitcast.74), kind=kOutput, calls=%fused_computation.49 | convolution fusion | flops 7340032 | bytes 1835136 | tf_op jit(solution)/shard_map/dot_general | solution.py:141
  223.4 72.6 %reduce-scatter.2.cloned.1.call-done = bf16[128,3584]{1,0:T(8,128)(2,1)} async-done(((bf16[2048,3584]{1,0:T(8,128)(2,1)}), bf16[128,3584]{1,0:T(8,128)(2,1)}) %reduce-scatter.2.cloned.1.call-update) | async-done | bytes 917520 | tf_op jit(solution)/shard_map/reduce_scatter | solution.py:122
  (80 shorter events, 11.9 us)
Async XLA Ops:
  7.2 86.0 %copy-start = (bf16[448,3584]{1,0:T(8,128)(2,1)S(1)}, bf16[448,3584]{1,0:T(8,128)(2,1)}, u32[]{:S(2)}) copy-start(bf16[448,3584]{1,0:T(8,128)(2,1)} %param.19) | copy-start | bytes 9633796
  7.2 14.7 %copy-start.8 = (f32[1,2048,7]{1,0,2:T(1,128)S(1)}, f32[1,2048,7]{1,0,2:T(1,128)}, u32[]{:S(2)}) copy-start(f32[1,2048,7]{1,0,2:T(1,128)} %param.15) | copy-start | bytes 172036
  7.2 288.8 %reduce-scatter.2.cloned.1.call-start = ((), (), s32[]{:S(2)}) async-start(), calls=%async_computation.2 | async-start | bytes 15597568 | tf_op jit(solution)/shard_map/reduce_scatter | solution.py:122
  13.3 0.6 copy-start.5
  26.6 3.8 %copy-start.7 = (f32[2048,7]{0,1:T(8,128)S(1)}, f32[2048,7]{0,1:T(8,128)}, u32[]{:S(2)}) copy-start(f32[2048,7]{0,1:T(8,128)} %reduce.3) | copy-start | bytes 172036
  26.6 3.8 %copy-start.10 = (f32[8,256]{1,0:T(8,128)S(1)}, f32[8,256]{1,0:T(8,128)}, u32[]{:S(2)}) copy-start(f32[8,256]{1,0:T(8,128)} %get-tuple-element.7) | copy-start | bytes 24580
  26.6 3.8 %copy-start.11 = (f32[8,256]{1,0:T(8,128)S(1)}, f32[8,256]{1,0:T(8,128)}, u32[]{:S(2)}) copy-start(f32[8,256]{1,0:T(8,128)} %get-tuple-element.8) | copy-start | bytes 24580
  26.6 3.9 %copy-start.1 = (bf16[56,8,8,256]{3,2,1,0:T(8,128)(2,1)S(1)}, bf16[56,8,8,256]{3,2,1,0:T(8,128)(2,1)}, u32[]{:S(2)}) copy-start(bf16[56,8,8,256]{3,2,1,0:T(8,128)(2,1)} %copy.208) | copy-start | bytes 5505028
  36.1 6.2 %copy-start.4 = (bf16[1,2048,448]{1,2,0:T(8,128)(2,1)S(1)}, bf16[1,2048,448]{1,2,0:T(8,128)(2,1)}, u32[]{:S(2)}) copy-start(bf16[1,2048,448]{1,2,0:T(8,128)(2,1)} %param.12) | copy-start | bytes 5505028
  45.1 0.7 copy-start.13
  45.1 2.5 copy-start.3
  47.7 0.7 copy-start.16
  53.2 40.0 %copy-start.15 = (f32[448]{0:T(512)S(1)}, f32[448]{0:T(512)}, u32[]{:S(2)}) copy-start(f32[448]{0:T(512)} %param.18) | copy-start | bytes 5380
  108.4 0.7 copy-start.9
  108.4 0.8 copy-start.6
  108.4 2.3 copy-start.2
  117.4 6.8 %copy-start.14 = (s32[8]{0:T(128)S(1)}, s32[8]{0:T(128)}, u32[]{:S(2)}) copy-start(s32[8]{0:T(128)} %get-tuple-element.11) | copy-start | bytes 100
  120.8 13.6 %copy-start.12 = (s32[16,8]{0,1:T(8,128)S(1)}, s32[16,8]{0,1:T(8,128)}, u32[]{:S(2)}) copy-start(s32[16,8]{0,1:T(8,128)} %param.21) | copy-start | bytes 1540
  128.0 92.2 %all-to-all-start = ((bf16[16,7,4096]{2,1,0:T(8,128)(2,1)}), bf16[16,7,4096]{2,1,0:T(8,128)(2,1)}, u32[]{:S(2)}, u32[]{:S(2)}) async-start(bf16[16,7,4096]{2,1,0:T(8,128)(2,1)} %copy.179), calls=%async_computation.1 | async-start | bytes 2097152 | tf_op jit(solution)/shard_map/all_to_all | solution.py:136
Sparse Core Ops, SparseCore 0:
  108.5 187.4 reduce-scatter.1
